TPU v7x, 32 devices: a whole 2x2x4 slice. The times are simulated.
32 devices in a mesh: grp: 2 (over x), cand: 8 (over z, y), seq: 2 (over core).
Axes of the slice: x: 2, y: 2, z: 4, core: 2. Of those that a mesh axis runs over, the one named last changes fastest.
Arguments:
- x_prefix: bfloat16 [8192, 2560], P(('grp', 'cand', 'seq')), parts along dimension 0, may hold values from -6 to 6
- b_prefix: bfloat16 [8192, 128], P(('grp', 'cand', 'seq')), parts along dimension 0, may hold values from -0.5 to 0.5
- code_prefix: int32 [8192, 40], P(('grp', 'cand', 'seq')), parts along dimension 0, may hold values from 0 to 500
- x_cand: bfloat16 [32, 512, 2560], P(('grp', 'cand'), None, 'seq'), parts along dimension 0, may hold values from -6 to 6
- b_cand: bfloat16 [32, 512, 128], P(('grp', 'cand')), parts along dimension 0, may hold values from -0.5 to 0.5
- c_cand: bfloat16 [32, 512, 128], P(('grp', 'cand')), parts along dimension 0, may hold values from -0.5 to 0.5
- code_cand: int32 [32, 512, 40], P(('grp', 'cand'), None, 'seq'), parts along dimension 0, may hold values from 0 to 500
- lengths: int32 [32], P(('grp', 'cand')), parts along dimension 0, may hold values from 1 to 2, as said below
- dy_cand: bfloat16 [32, 512, 2560], P(('grp', 'cand'), None, 'seq'), parts along dimension 0, may hold values from -1.5 to 1.5
Outputs:
- dx_prefix: bfloat16 [8192, 2560], P(('grp', 'cand', 'seq')), parts along dimension 0
- db_prefix: float32 [8192, 128], P(('grp', 'cand', 'seq')), parts along dimension 0
- dx_cand: bfloat16 [32, 512, 2560], P(('grp', 'cand'), None, 'seq'), parts along dimension 0
- db_cand: float32 [32, 512, 128], P(('grp', 'cand'), 'seq'), parts along dimension 0
- dc_cand: float32 [32, 512, 128], P(('grp', 'cand'), 'seq'), parts along dimension 0
There are 2 independent parts, one for each index of `grp`. A program takes and returns all parts, laid end to end along the dimension named above; each array names one. Nothing has to cross between parts.
Inputs may be any that keep to these rules, and one draw needn't show every extreme that they name: lengths count blocks of 256 tokens.
All inputs are finite; a program needn't handle non-finite values.
Results may differ from a plain program's by a relative error of at most 0.0015.
The roundings to bfloat16 on the way count: a program that leaves them out, or rounds other values in their place, can miss the bound.
Values may be sent and summed in bfloat16 or wider, within the bound.
No kernel may reach another device: no remote copies, remote signals or barrier semaphores. Data moves between devices by JAX's collectives and lax.ppermute only.
A program may use at most 256 MiB of HBM per device.

v0:
```python
import jax
import jax.numpy as jnp
from jax import lax
from jax.sharding import PartitionSpec as P

BLOCK = 256


def split_bf16(value):
    high = lax.reduce_precision(value, exponent_bits=8, mantissa_bits=7)
    low = (value - high).astype(jnp.bfloat16)
    return (high.astype(jnp.bfloat16), low)


def shards(x_prefix, b_prefix, code_prefix, x_cand, b_cand, c_cand, code_cand, lengths, dy_cand):
    pre_len, width = x_prefix.shape
    heads_total = code_prefix.shape[1]
    head_size = width // heads_total
    nstate = b_prefix.shape[1]
    cand_dev, cand_len, half_width = x_cand.shape
    half_heads = code_cand.shape[2]
    pre_axes = ("cand", "seq")
    log_prefix = jnp.log1p(-code_prefix.astype(jnp.float32) * 1e-06)
    own_total = jnp.sum(log_prefix, axis=0)
    shard_count = lax.axis_size(pre_axes)
    mine = lax.axis_index(pre_axes)
    shard_at = jnp.arange(shard_count, dtype=jnp.int32)
    lanes = -(-heads_total // 128) * 128
    padded = jnp.pad(own_total, (0, lanes - heads_total))
    rows = jnp.where((shard_at < mine)[:, None], padded[None, :], 0.0)
    rows = jnp.broadcast_to(rows[:, None, :], (shard_count, 8, lanes))
    later_total = lax.psum_scatter(rows, pre_axes, scatter_dimension=0, tiled=True)
    later_total = later_total[0, 0, :heads_total]
    after_local = own_total[None, :] - jnp.cumsum(log_prefix, axis=0)
    weight = jnp.exp(after_local + later_total[None, :])
    weighted_b = (weight[:, :, None] * b_prefix[:, None, :].astype(jnp.float32)).astype(
        jnp.bfloat16
    )
    x_heads = x_prefix.reshape(pre_len, heads_total, head_size)
    state_full = jnp.einsum("jhp,jhn->hpn", x_heads, weighted_b, preferred_element_type=jnp.float32)
    seq_at = lax.axis_index("seq")
    traced_zero = later_total[0] * 0.0
    init_full = lax.psum(state_full, pre_axes) + traced_zero
    init_half = lax.dynamic_slice_in_dim(init_full, seq_at * half_heads, half_heads, 0)
    init_half = init_half.astype(jnp.bfloat16)
    position = jnp.arange(cand_len, dtype=jnp.int32)
    valid_rows = position[None, :] < lengths[:, None] * BLOCK
    g_cand = jnp.where(valid_rows[:, :, None], dy_cand, jnp.zeros_like(dy_cand))
    level_all = jnp.cumsum(jnp.log1p(-code_cand.astype(jnp.float32) * 1e-06), axis=1)
    amplitude = jnp.exp(level_all)
    inverse = jnp.exp(-level_all)
    g_heads = g_cand.reshape(cand_dev, cand_len, half_heads, head_size)
    xc_heads = x_cand.reshape(cand_dev, cand_len, half_heads, head_size)
    scaled_g = g_heads.astype(jnp.float32) * amplitude[:, :, :, None]
    decayed_g, g_low = split_bf16(scaled_g)
    x_high, x_low = split_bf16(xc_heads.astype(jnp.float32) * inverse[:, :, :, None])
    dstate = jnp.einsum("cthp,ctn->hpn", decayed_g, c_cand, preferred_element_type=jnp.float32)
    grad_half = (lax.psum(dstate, "cand") + traced_zero).astype(jnp.bfloat16)
    grad_state = lax.all_gather(grad_half, "seq", axis=0, tiled=True)
    causal = position[:, None] >= position[None, :]
    flat = (cand_dev, cand_len, half_width)

    def pair(left, right):
        return jnp.einsum(
            "ctk,csk->cts",
            left.reshape(flat),
            right.reshape(flat),
            preferred_element_type=jnp.float32,
        )

    weight_sum = pair(decayed_g, x_high) + pair(decayed_g, x_low) + pair(g_low, x_high)
    weight_sum = jnp.where(causal[None], weight_sum, 0.0)
    db_part = jnp.einsum(
        "cts,ctn->csn", weight_sum, c_cand.astype(jnp.float32), precision=lax.Precision.HIGHEST
    )
    dc_part = jnp.einsum(
        "cts,csn->ctn", weight_sum, b_cand.astype(jnp.float32), precision=lax.Precision.HIGHEST
    )
    scores = jnp.einsum("ctn,csn->cts", c_cand, b_cand, preferred_element_type=jnp.float32)
    amp_t = jnp.transpose(amplitude, (0, 2, 1))
    inv_t = jnp.transpose(inverse, (0, 2, 1))
    decay_mat = amp_t[:, :, :, None] * inv_t[:, :, None, :]
    kernel = jnp.where(causal[None, None], scores[:, None] * decay_mat, 0.0).astype(jnp.bfloat16)
    dx_cand = jnp.einsum("chts,cthp->cshp", kernel, g_heads, preferred_element_type=jnp.float32)
    dx_cand = dx_cand.astype(jnp.bfloat16).reshape(flat)
    dc_state = jnp.dot(
        decayed_g.reshape(cand_dev * cand_len, half_width),
        init_half.reshape(half_width, nstate),
        preferred_element_type=jnp.float32,
    )
    dc_total = dc_part + dc_state.reshape(cand_dev, cand_len, nstate)
    db_cand = lax.psum_scatter(db_part, "seq", scatter_dimension=1, tiled=True)
    dc_cand = lax.psum_scatter(dc_total, "seq", scatter_dimension=1, tiled=True)
    dx_prefix = jnp.einsum(
        "jhn,hpn->jhp", weighted_b, grad_state, preferred_element_type=jnp.float32
    )
    dx_prefix = dx_prefix.astype(jnp.bfloat16).reshape(pre_len, width)
    projected = jnp.einsum("jhp,hpn->jhn", x_heads, grad_state, preferred_element_type=jnp.float32)
    db_prefix = jnp.sum(projected * weight[:, :, None], axis=1)
    return (dx_prefix, db_prefix, dx_cand, db_cand, dc_cand)


def solution(mesh):
    return jax.shard_map(
        shards,
        mesh=mesh,
        in_specs=(
            P(("grp", "cand", "seq"), None),
            P(("grp", "cand", "seq"), None),
            P(("grp", "cand", "seq"), None),
            P(("grp", "cand"), None, "seq"),
            P(("grp", "cand"), None, None),
            P(("grp", "cand"), None, None),
            P(("grp", "cand"), None, "seq"),
            P(("grp", "cand")),
            P(("grp", "cand"), None, "seq"),
        ),
        out_specs=(
            P(("grp", "cand", "seq"), None),
            P(("grp", "cand", "seq"), None),
            P(("grp", "cand"), None, "seq"),
            P(("grp", "cand"), "seq", None),
            P(("grp", "cand"), "seq", None),
        ),
        check_vma=False,
    )
```

profile of v0, /device:TPU:0, one launch (start us, length us, event | category | flops | bytes accessed | tf_op | source)
XLA Modules:
  0.0 305.6 jit_solution(1528307880977346940)
XLA Ops:
  10.1 2.3 reduce-window.14
  13.6 2.4 copy.63
  16.8 82.5 %all-reduce.10.cloned.1.call-done = f32[16,8,128]{2,1,0:T(8,128)} async-done(((f32[16,8,128]{2,1,0:T(8,128)}), f32[16,8,128]{2,1,0:T(8,128)}) %all-reduce.10.cloned.1.call-update) | async-done | bytes 65552
  101.3 3.5 %fusion.19 = f32[40,64,128]{2,1,0:T(8,128)} fusion(bf16[256,40,64]{0,2,1:T(8,128)(2,1)} %bitcast.91, f32[256,128]{0,1:T(8,128)S(1)} %copy.61, f32[256,40]{0,1:T(8,128)S(1)} %fusion.25), kind=kOutput, calls=%fused_computation.31 | convolution fusion | flops 170393600 | bytes 2793472 | tf_op jit(solution)/shard_map/jhp,jhn->hpn/dot_general | solution.py:40
  105.2 2.6 copy.55
  107.9 4.4 %copy.67 = bf16[2,512,1280]{1,2,0:T(8,128)(2,1)} copy(bf16[2,512,1280]{2,1,0:T(8,128)(2,1)} %param.12) | data formatting | bytes 5242880 | tf_op args[3]
  112.4 5.7 %fusion.6 = (bf16[2,512,1280]{1,2,0:T(8,128)(2,1)}, bf16[2,512,1280]{1,2,0:T(8,128)(2,1)S(1)}, bf16[2,512,1280]{1,2,0:T(8,128)(2,1)}, bf16[2,512,1280]{1,2,0:T(8,128)(2,1)}) fusion(f32[2,512,20]{1,2,0:T(8,128)S(1)} %copy.58, bf16[2,512,1280]{1,2,0:T(8,128)(2,1)} %copy.55, pred[2,512]{1,0:T(4,128)(4,1)S(1)} %iota_compare_fusion.1, ...), kind=kLoop, calls=%fused_computation.11 | loop fusion | flops 15728640 | bytes 15893504 | tf_op jit(solution)/shard_map/convert_element_type | solution.py:11
  118.0 1.7 fusion.20
  120.7 1.7 copy-done.5
  122.4 1.6 fusion.30
  124.2 1.6 fusion.31
  125.9 1.8 add_select_fusion
  127.7 2.7 fusion.32
  130.7 1.8 fusion.29
  132.5 1.9 fusion.33
  135.6 64.6 %all-reduce.8.cloned.1.call-done = f32[40,64,128]{2,1,0:T(8,128)} async-done(((f32[40,64,128]{2,1,0:T(8,128)}), f32[40,64,128]{2,1,0:T(8,128)}) %all-reduce.8.cloned.1.call-update) | async-done | bytes 1310736 | tf_op jit(solution)/shard_map/psum | solution.py:43
  201.5 3.5 %convolution_add_fusion = f32[2,512,128]{2,1,0:T(8,128)} fusion(f32[2,512,128]{2,1,0:T(8,128)} %fusion.33, bf16[2,512,1280]{1,2,0:T(8,128)(2,1)} %copy-done.3, bf16[1280,128,1]{1,0,2:T(8,128)(2,1)S(1)} %bitcast.94), kind=kOutput, calls=%fused_computation.33 | convolution fusion | flops 335675392 | bytes 3997696 | tf_op jit(solution)/shard_map/dot_general | solution.py:86
  205.0 7.7 %fusion.17 = bf16[2,20,64,512]{3,2,1,0:T(8,128)(2,1)} fusion(bf16[2,512,20,64]{1,3,2,0:T(8,128)(2,1)S(1)} %bitcast.89, f32[2,20,512]{2,1,0:T(8,128)S(1)} %copy.66, f32[2,20,512]{2,1,0:T(8,128)S(1)} %copy.64, f32[2,512,512]{2,1,0:T(8,128)} %fusion.29, pred[512,512]{1,0:T(8,128)(4,1)S(1)} %iota_compare_fusion), kind=kOutput, calls=%fused_computation.29 | convolution fusion | flops 1385431040 | bytes 7766016 | tf_op jit(solution)/shard_map/chts,cthp->cshp/dot_general | solution.py:84
  212.8 4.4 %copy.80 = bf16[2,512,1280]{2,1,0:T(8,128)(2,1)} copy(bf16[2,512,1280]{1,2,0:T(8,128)(2,1)} %bitcast.90) | data formatting | bytes 5242880
  217.1 60.1 %all-reduce.6.cloned.1.call-done = f32[20,64,128]{2,1,0:T(8,128)} async-done(((f32[20,64,128]{2,1,0:T(8,128)}), f32[20,64,128]{2,1,0:T(8,128)}) %all-reduce.6.cloned.1.call-update) | async-done | bytes 655376 | tf_op jit(solution)/shard_map/psum | solution.py:58
  278.4 2.3 all_gather.3
  282.3 1.6 copy.78
  283.8 1.7 fusion.8
  287.2 11.9 %reduce-scatter.5.cloned.1.call-done = f32[2,256,128]{2,1,0:T(8,128)} async-done(((f32[2,512,128]{2,1,0:T(8,128)}), f32[2,256,128]{2,1,0:T(8,128)}) %reduce-scatter.5.cloned.1.call-update) | async-done | bytes 262160 | tf_op jit(solution)/shard_map/reduce_scatter | solution.py:93
  (79 shorter events, 14.8 us)
Async XLA Ops:
  7.2 110.9 %copy-start = (bf16[2,512,128]{2,1,0:T(8,128)(2,1)S(1)}, bf16[2,512,128]{2,1,0:T(8,128)(2,1)}, u32[]{:S(2)}) copy-start(bf16[2,512,128]{2,1,0:T(8,128)(2,1)} %param.14) | copy-start | bytes 786436
  7.2 9.0 %copy-start.14 = (u32[32]{0:T(128)S(1)}, u32[32]{0:T(128)}, u32[]{:S(2)}) copy-start(u32[32]{0:T(128)} %constant.44) | copy-start | bytes 388
  7.2 8.9 %copy-start.11 = (bf16[256,128]{1,0:T(8,128)(2,1)S(1)}, bf16[256,128]{1,0:T(8,128)(2,1)}, u32[]{:S(2)}) copy-start(bf16[256,128]{1,0:T(8,128)(2,1)} %param.10) | copy-start | bytes 196612
  7.2 92.1 %all-reduce.10.cloned.1.call-start = ((), (), s32[]{:S(2)}) async-start(), calls=%async_computation.6 | async-start | bytes 131072
  9.0 191.2 %all-reduce.8.cloned.1.call-start = ((), (), s32[]{:S(2)}) async-start(), calls=%async_computation.4 | async-start | bytes 2621440 | tf_op jit(solution)/shard_map/psum | solution.py:43
  16.1 88.9 %copy-start.13 = (s32[2]{0:T(128)S(1)}, s32[2]{0:T(128)}, u32[]{:S(2)}) copy-start(s32[2]{0:T(128)} %param.16) | copy-start | bytes 28
  16.2 88.8 %copy-start.10 = (f32[256,128]{0,1:T(8,128)}, f32[256,128]{0,1:T(8,128)S(1)}, u32[]{:S(2)}) copy-start(f32[256,128]{0,1:T(8,128)S(1)} %copy.61) | copy-start | bytes 393220
  100.7 0.6 copy-start.12
  101.3 3.9 %copy-start.7 = (bf16[2,512,1280]{2,1,0:T(8,128)(2,1)S(1)}, bf16[2,512,1280]{2,1,0:T(8,128)(2,1)}, u32[]{:S(2)}) copy-start(bf16[2,512,1280]{2,1,0:T(8,128)(2,1)} %param.17) | copy-start | bytes 7864324
  104.9 172.4 %all-reduce.6.cloned.1.call-start = ((), (), s32[]{:S(2)}) async-start(), calls=%async_computation.2 | async-start | bytes 1310720 | tf_op jit(solution)/shard_map/psum | solution.py:58
  118.0 2.0 copy-start.1
  119.8 167.4 %reduce-scatter.3.cloned.1.call-start = ((), (), s32[]{:S(2)}) async-start(), calls=%async_computation.3 | async-start | bytes 786432 | tf_op jit(solution)/shard_map/reduce_scatter | solution.py:92
  120.0 2.4 copy-start.5
  120.6 3.4 %copy-start.3 = (bf16[2,512,1280]{1,2,0:T(8,128)(2,1)}, bf16[2,512,1280]{1,2,0:T(8,128)(2,1)S(1)}, u32[]{:S(2)}) copy-start(bf16[2,512,1280]{1,2,0:T(8,128)(2,1)S(1)} %reduce-precision_convert_fusion.1) | copy-start | bytes 7864324
  122.4 1.8 copy-start.6
  124.2 1.7 copy-start.4
  127.7 3.0 copy-start.9
  130.4 168.7 %reduce-scatter.5.cloned.1.call-start = ((), (), s32[]{:S(2)}) async-start(), calls=%async_computation.5 | async-start | bytes 786432 | tf_op jit(solution)/shard_map/reduce_scatter | solution.py:93
  200.2 4.9 %copy-start.2 = (bf16[2,512,1280]{1,2,0:T(8,128)(2,1)S(1)}, bf16[2,512,1280]{1,2,0:T(8,128)(2,1)}, u32[]{:S(2)}) copy-start(bf16[2,512,1280]{1,2,0:T(8,128)(2,1)} %copy-done.1) | copy-start | bytes 7864324
  280.7 3.1 %copy-start.8 = (bf16[256,2560]{0,1:T(8,128)(2,1)S(1)}, bf16[256,2560]{0,1:T(8,128)(2,1)}, u32[]{:S(2)}) copy-start(bf16[256,2560]{0,1:T(8,128)(2,1)} %copy.63) | copy-start | bytes 3932164
Sparse Core Ops, SparseCore 0:
  12.1 87.1 all-reduce.9
  105.0 95.1 all-reduce.7
  204.0 73.2 all-reduce.5
  280.0 7.2 reduce-scatter.2
  290.0 9.0 reduce-scatter.4
where the time goes:
time: 306 us
  waiting for transfers between devices  220 us (72%)
  matrix products  31 us (10%)
  local copies, waits for them, and re-layouts  22.8 us (7%)
  between operations  14.8 us (5%)
  other arithmetic  14 us (5%)
    unnamed x6, waiting for transfers between devices  82.6 us
    psum x1, waiting for transfers between devices, shards(): init_full = lax.psum(state_full, pre_axes) + traced_zero  64.6 us
    psum x1, waiting for transfers between devices, shards(): grad_half = (lax.psum(dstate, 'cand') + traced_zero).astype(jnp.bfloat16)  60.1 us
    unnamed x38, local copies, waits for them, and re-layouts  20.8 us
    reduce_scatter x1, waiting for transfers between devices, shards(): dc_cand = lax.psum_scatter(dc_total, 'seq', scatter_dimension=1, tiled=True)  11.9 us
    dot_general x1, matrix products, shards(): jnp.einsum('chts,cthp->cshp', kernel, g_heads, preferred_element_type=jnp...  7.72 us
  transfers between devices with their start and end apart: 5, of which 5 were waited for; matrix products, arithmetic and copies ran while one was open for 19% of the time, Pallas kernels for 0%

commit v1 on v0

--- a/solution.py
+++ b/solution.py
@@ -40,7 +40,7 @@
     state_full = jnp.einsum("jhp,jhn->hpn", x_heads, weighted_b, preferred_element_type=jnp.float32)
     seq_at = lax.axis_index("seq")
     traced_zero = later_total[0] * 0.0
-    init_full = lax.psum(state_full, pre_axes) + traced_zero
+    init_full = jnp.sum(lax.all_gather(state_full, pre_axes), axis=0) + traced_zero
     init_half = lax.dynamic_slice_in_dim(init_full, seq_at * half_heads, half_heads, 0)
     init_half = init_half.astype(jnp.bfloat16)
     position = jnp.arange(cand_len, dtype=jnp.int32)

time: 306 us -> 278 us (0.908)
  waiting for transfers between devices: 220 us -> 184 us
  other arithmetic: 14 us -> 22.3 us
  matrix products: 31 us -> 27.7 us
    all_gather x0 -> x1, waiting for transfers between devices: none -> 85 us  [shards(): lax.all_gather(state_full, pre_axes)]
    psum x1 -> x0, waiting for transfers between devices: 64.6 us -> none  [shards(): init_full = lax.psum(state_full, pre_axes) + traced_zero]
    psum x1, waiting for transfers between devices: 60.1 us -> 12.7 us  [shards(): grad_half = (lax.psum(dstate, 'cand') + traced_zero).astype(jnp.bfloat16)]
    reduce_scatter x1, waiting for transfers between devices: 11.9 us -> 0.01 us  [shards(): dc_cand = lax.psum_scatter(dc_total, 'seq', scatter_dimension=1, tiled=True)]
    reduce_sum x0 -> x1, other arithmetic: none -> 9.14 us  [shards(): jnp.sum(lax.all_gather(state_full, pre_axes), axis=0) + traced_zero]
    unnamed x6, waiting for transfers between devices: 82.6 us -> 86.8 us
    unnamed x38 -> x44, local copies, waits for them, and re-layouts: 20.8 us -> 20 us
  transfers between devices with their start and end apart: 5 -> 5, of which waited for: 5 -> 3; matrix products, arithmetic and copies ran while one was open for 19% -> 24% of each run, Pallas kernels for 0% -> 0%
where the time goes in v1:
time: 278 us; the launch traced here: 277 us
  waiting for transfers between devices  184 us (66%)
  matrix products  27.7 us (10%)
  local copies, waits for them, and re-layouts  23.4 us (8%)
  other arithmetic  22.3 us (8%)
  between operations  16.2 us (6%)
    unnamed x6, waiting for transfers between devices  86.8 us
    all_gather x1, waiting for transfers between devices, shards(): lax.all_gather(state_full, pre_axes)  85 us
    unnamed x44, local copies, waits for them, and re-layouts  20 us
    psum x1, waiting for transfers between devices, shards(): grad_half = (lax.psum(dstate, 'cand') + traced_zero).astype(jnp.bfloat16)  12.7 us
    reduce_sum x1, other arithmetic, shards(): jnp.sum(lax.all_gather(state_full, pre_axes), axis=0) + traced_zero  9.14 us
    dot_general x1, matrix products, shards(): jnp.einsum('chts,cthp->cshp', kernel, g_heads, preferred_element_type=jnp...  7.72 us
    convert_element_type x1, other arithmetic, split_bf16(): low = (value - high).astype(jnp.bfloat16)  5.66 us
  transfers between devices with their start and end apart: 5, of which 3 were waited for; matrix products, arithmetic and copies ran while one was open for 24% of the time, Pallas kernels for 0%

profile of v1, /device:TPU:0, one launch (start us, length us, event | category | flops | bytes accessed | tf_op | source)
XLA Modules:
  0.0 276.9 jit_solution(2644112052217907883)
XLA Ops:
  11.6 1.6 copy.63
  13.8 86.7 %all-reduce.7.cloned.1.call-done = f32[16,8,128]{2,1,0:T(8,128)} async-done(((f32[16,8,128]{2,1,0:T(8,128)}), f32[16,8,128]{2,1,0:T(8,128)}) %all-reduce.7.cloned.1.call-update) | async-done | bytes 65552
  100.5 1.3 constant_dynamic-slice_fusion
  101.9 2.1 fusion.19
  104.4 2.3 reduce-window.14
  107.3 2.7 copy.67
  110.0 4.6 %copy.55 = bf16[2,512,1280]{1,2,0:T(8,128)(2,1)} copy(bf16[2,512,1280]{2,1,0:T(8,128)(2,1)} %param.17) | data formatting | bytes 5242880 | tf_op args[8]
  114.6 5.7 %fusion.6 = (bf16[2,512,1280]{1,2,0:T(8,128)(2,1)}, bf16[2,512,1280]{1,2,0:T(8,128)(2,1)S(1)}, bf16[2,512,1280]{1,2,0:T(8,128)(2,1)}, bf16[2,512,1280]{1,2,0:T(8,128)(2,1)}) fusion(f32[2,512,20]{1,2,0:T(8,128)S(1)} %copy.58, bf16[2,512,1280]{1,2,0:T(8,128)(2,1)} %copy.55, pred[2,512]{1,0:T(4,128)(4,1)S(1)} %iota_compare_fusion.1, ...), kind=kLoop, calls=%fused_computation.11 | loop fusion | flops 15728640 | bytes 15893504 | tf_op jit(solution)/shard_map/convert_element_type | solution.py:11
  120.3 1.7 fusion.20
  123.0 1.9 copy-done.7
  124.8 1.6 fusion.31
  126.6 1.6 fusion.30
  128.4 1.8 add_select_fusion
  130.2 2.7 fusion.32
  133.8 1.8 fusion.29
  135.6 1.9 fusion.33
  138.6 85.0 %all-gather.3.cloned.1.call-done = f32[640,64,128]{2,1,0:T(8,128)} async-done(((f32[40,64,128]{2,1,0:T(8,128)}), f32[640,64,128]{2,1,0:T(8,128)}) %all-gather.3.cloned.1.call-update) | async-done | bytes 20971536 | tf_op jit(solution)/shard_map/all_gather | solution.py:43
  223.6 9.1 %reduce_sum.29 = f32[40,64,128]{2,1,0:T(8,128)} reduce(f32[16,40,64,128]{3,2,1,0:T(8,128)} %bitcast.89, f32[]{:T(128)} %constant.14.clone.1), dimensions={0}, to_apply=%region_9.10 | reduce | flops 4915200 | bytes 22282244 | tf_op jit(solution)/shard_map/reduce_sum | solution.py:43
  234.1 3.6 %convolution_add_fusion = f32[2,512,128]{2,1,0:T(8,128)} fusion(f32[2,512,128]{2,1,0:T(8,128)} %fusion.33, bf16[2,512,1280]{1,2,0:T(8,128)(2,1)} %copy-done.4, bf16[1280,128,1]{1,0,2:T(8,128)(2,1)S(1)} %bitcast.96), kind=kOutput, calls=%fused_computation.33 | convolution fusion | flops 335675392 | bytes 3997696 | tf_op jit(solution)/shard_map/dot_general | solution.py:86
  237.6 7.7 %fusion.17 = bf16[2,20,64,512]{3,2,1,0:T(8,128)(2,1)} fusion(bf16[2,512,20,64]{1,3,2,0:T(8,128)(2,1)S(1)} %bitcast.91, f32[2,20,512]{2,1,0:T(8,128)S(1)} %copy-done.12, f32[2,20,512]{2,1,0:T(8,128)S(1)} %copy.64, f32[2,512,512]{2,1,0:T(8,128)} %fusion.29, pred[512,512]{1,0:T(8,128)(4,1)S(1)} %iota_compare_fusion), kind=kOutput, calls=%fused_computation.29 | convolution fusion | flops 1385431040 | bytes 7766016 | tf_op jit(solution)/shard_map/chts,cthp->cshp/dot_general | solution.py:84
  245.4 4.5 %copy.80 = bf16[2,512,1280]{2,1,0:T(8,128)(2,1)} copy(bf16[2,512,1280]{1,2,0:T(8,128)(2,1)} %bitcast.92) | data formatting | bytes 5242880
  249.9 12.7 %all-reduce.5.cloned.1.call-done = f32[20,64,128]{2,1,0:T(8,128)} async-done(((f32[20,64,128]{2,1,0:T(8,128)}), f32[20,64,128]{2,1,0:T(8,128)}) %all-reduce.5.cloned.1.call-update) | async-done | bytes 655376 | tf_op jit(solution)/shard_map/psum | solution.py:58
  263.7 2.3 all_gather.9
  268.2 1.6 copy.78
  (86 shorter events, 12.5 us)
Async XLA Ops:
  8.0 112.3 %copy-start = (bf16[2,512,128]{2,1,0:T(8,128)(2,1)S(1)}, bf16[2,512,128]{2,1,0:T(8,128)(2,1)}, u32[]{:S(2)}) copy-start(bf16[2,512,128]{2,1,0:T(8,128)(2,1)} %param.14) | copy-start | bytes 786436
  8.0 5.2 %copy-start.17 = (u32[32]{0:T(128)S(1)}, u32[32]{0:T(128)}, u32[]{:S(2)}) copy-start(u32[32]{0:T(128)} %constant.44) | copy-start | bytes 388
  8.0 92.5 %all-reduce.7.cloned.1.call-start = ((), (), s32[]{:S(2)}) async-start(), calls=%async_computation.6 | async-start | bytes 131072
  9.8 213.8 %all-gather.3.cloned.1.call-start = ((), (), s32[]{:S(2)}) async-start(), calls=%async_computation.5 | async-start | bytes 22282240 | tf_op jit(solution)/shard_map/all_gather | solution.py:43
  13.2 88.7 %copy-start.9 = (bf16[256,2560]{0,1:T(8,128)(2,1)}, bf16[256,2560]{0,1:T(8,128)(2,1)S(1)}, u32[]{:S(2)}) copy-start(bf16[256,2560]{0,1:T(8,128)(2,1)S(1)} %copy.63) | copy-start | bytes 3932164
  13.2 90.9 %copy-start.13 = (s32[2,512,20]{1,0,2:T(2,128)S(1)}, s32[2,512,20]{1,0,2:T(2,128)}, u32[]{:S(2)}) copy-start(s32[2,512,20]{1,0,2:T(2,128)} %param.15) | copy-start | bytes 245764
  101.9 2.1 copy-start.14
  104.0 3.3 %copy-start.8 = (bf16[2,512,1280]{2,1,0:T(8,128)(2,1)S(1)}, bf16[2,512,1280]{2,1,0:T(8,128)(2,1)}, u32[]{:S(2)}) copy-start(bf16[2,512,1280]{2,1,0:T(8,128)(2,1)} %param.12) | copy-start | bytes 7864324
  104.1 158.5 %all-reduce.5.cloned.1.call-start = ((), (), s32[]{:S(2)}) async-start(), calls=%async_computation.2 | async-start | bytes 1310720 | tf_op jit(solution)/shard_map/psum | solution.py:58
  110.0 4.6 %copy-start.16 = (s32[2]{0:T(128)S(1)}, s32[2]{0:T(128)}, u32[]{:S(2)}) copy-start(s32[2]{0:T(128)} %param.16) | copy-start | bytes 28
  120.3 2.1 copy-start.2
  122.1 147.7 %reduce-scatter.3.cloned.1.call-start = ((), (), s32[]{:S(2)}) async-start(), calls=%async_computation.3 | async-start | bytes 786432 | tf_op jit(solution)/shard_map/reduce_scatter | solution.py:92
  122.4 2.4 copy-start.7
  122.9 3.5 %copy-start.4 = (bf16[2,512,1280]{1,2,0:T(8,128)(2,1)}, bf16[2,512,1280]{1,2,0:T(8,128)(2,1)S(1)}, u32[]{:S(2)}) copy-start(bf16[2,512,1280]{1,2,0:T(8,128)(2,1)S(1)} %reduce-precision_convert_fusion.1) | copy-start | bytes 7864324
  124.8 1.8 copy-start.6
  126.6 1.8 copy-start.5
  130.2 3.6 %copy-start.11 = (bf16[2,512,128]{2,1,0:T(8,128)(2,1)S(1)}, bf16[2,512,128]{2,1,0:T(8,128)(2,1)}, u32[]{:S(2)}) copy-start(bf16[2,512,128]{2,1,0:T(8,128)(2,1)} %param.13) | copy-start | bytes 786436
  132.9 136.9 %reduce-scatter.5.cloned.1.call-start = ((), (), s32[]{:S(2)}) async-start(), calls=%async_computation.4 | async-start | bytes 786432 | tf_op jit(solution)/shard_map/reduce_scatter | solution.py:93
  232.7 4.9 %copy-start.3 = (bf16[2,512,1280]{1,2,0:T(8,128)(2,1)S(1)}, bf16[2,512,1280]{1,2,0:T(8,128)(2,1)}, u32[]{:S(2)}) copy-start(bf16[2,512,1280]{1,2,0:T(8,128)(2,1)} %copy-done.2) | copy-start | bytes 7864324
  232.7 4.9 %copy-start.12 = (f32[2,20,512]{2,1,0:T(8,128)S(1)}, f32[2,20,512]{2,1,0:T(8,128)}, u32[]{:S(2)}) copy-start(f32[2,20,512]{2,1,0:T(8,128)} %copy.66) | copy-start | bytes 245764
  245.4 20.6 %copy-start.10 = (bf16[256,2560]{0,1:T(8,128)(2,1)S(1)}, bf16[256,2560]{0,1:T(8,128)(2,1)}, u32[]{:S(2)}) copy-start(bf16[256,2560]{0,1:T(8,128)(2,1)} %copy-done.9) | copy-start | bytes 3932164
  245.4 20.6 %copy-start.15 = (f32[256,40]{0,1:T(8,128)S(1)}, f32[256,40]{0,1:T(8,128)}, u32[]{:S(2)}) copy-start(f32[256,40]{0,1:T(8,128)} %copy-done.14) | copy-start | bytes 122884
  266.0 3.8 %copy-start.1 = (bf16[2,512,128]{2,1,0:T(8,128)(2,1)S(1)}, bf16[2,512,128]{2,1,0:T(8,128)(2,1)}, u32[]{:S(2)}) copy-start(bf16[2,512,128]{2,1,0:T(8,128)(2,1)} %param.14) | copy-start | bytes 786436
Sparse Core Ops, SparseCore 0:
  13.3 87.1 all-reduce.6
  104.2 119.3 all-gather.2
  226.4 8.2 reduce-scatter.2
  237.8 8.7 reduce-scatter.4
Sparse Core Ops, SparseCore 1:
  122.1 140.4 all-reduce.4
